TPU v7x, 32 devices: a whole 2x2x4 slice. The times are simulated.
32 devices in a mesh: rep: 4 (over x, core), frame: 4 (over z), row: 2 (over y).
Axes of the slice: x: 2, y: 2, z: 4, core: 2. Of those that a mesh axis runs over, the one named last changes fastest.
Arguments:
- activations: bfloat16 [4, 4, 16, 32, 1280], P('rep', 'frame', 'row'), may hold values from -70 to 70, as said below
- spatial_weight: bfloat16 [9, 1280, 1280], P(None, None, ('rep', 'frame')), may hold values from -0.0546875 to 0.0546875
- temporal_weight: bfloat16 [3, 1280, 1280], P(None, None, ('rep', 'frame')), may hold values from -0.09375 to 0.09375
- first_gain: float32 [1280], replicated, may hold values from 0.25 to 1.75
- first_shift: float32 [1280], replicated, may hold values from -1.5 to 1.5
- spatial_bias: float32 [1280], replicated, may hold values from -2.5 to 2.5
- second_gain: float32 [1280], replicated, may hold values from 0.25 to 1.75
- second_shift: float32 [1280], replicated, may hold values from -1.5 to 1.5
- temporal_bias: float32 [1280], replicated, may hold values from -1.5 to 1.5
Outputs:
- block_out: float32 [4, 4, 16, 32, 1280], P('rep', 'frame', 'row')
Inputs may be any that keep to these rules, and one draw needn't show every extreme that they name: `activations`: finite values.
All inputs are finite; a program needn't handle non-finite values.
Results may differ from a plain program's by a relative error of at most 0.0009.
Values may be sent and summed in bfloat16 or wider, within the bound.
No kernel may reach another device: no remote copies, remote signals or barrier semaphores. Data moves between devices by JAX's collectives and lax.ppermute only.
A program may use at most 128 MiB of HBM per device.

v0:
```python
import numpy as np
import jax
import jax.numpy as jnp
from jax import lax
from jax.sharding import PartitionSpec as P

GROUPS = 32
EPS = 1e-05


def pair_sum(value, axis):
    if lax.axis_size(axis) == 2:
        return jax.tree.map(lambda v: v + lax.ppermute(v, axis, [(0, 1), (1, 0)]), value)
    return lax.psum(value, axis)


def gather_rep(w):
    size = lax.axis_size("rep")
    if size != 4:
        return lax.all_gather(w, "rep", axis=w.ndim - 1, tiled=True)
    index = lax.axis_index("rep")
    across = lax.ppermute(w, "rep", [(k, k ^ 2) for k in range(size)])
    partner = lax.ppermute(w, "rep", [(k, k ^ 1) for k in range(size)])
    diagonal = lax.ppermute(across, "rep", [(k, k ^ 1) for k in range(size)])
    held = [w, partner, across, diagonal]
    blocks = []
    for position in range(size):
        offset = index ^ position
        block = held[3]
        for d in (2, 1, 0):
            block = jnp.where(offset == d, held[d], block)
        blocks.append(block)
    return jnp.concatenate(blocks, axis=-1)


def local_vector(vec, frame_index, rep_size, frame_size):
    width = vec.shape[0] // (rep_size * frame_size)
    table = vec.reshape(rep_size, frame_size, width)
    return lax.dynamic_index_in_dim(table, frame_index, axis=1, keepdims=False).reshape(-1)


def silu_bf16(normed):
    return jax.nn.silu(normed).astype(jnp.bfloat16)


def temporal_wide(activations, second, temporal_w, temporal_bias):
    rep_size = lax.axis_size("rep")
    frame_size = lax.axis_size("frame")
    channels = activations.shape[-1]
    _, frames, rows, cols, local = second.shape
    shard_width = local // rep_size
    second_all = lax.all_gather(second, "frame", axis=4, tiled=True)
    rows_order = np.arange(channels).reshape(rep_size, frame_size, shard_width)
    rows_order = rows_order.transpose(1, 0, 2).reshape(-1)
    temporal_w = temporal_w[:, rows_order, :]
    lhs_t = second_all.reshape(frames, rows * cols, channels)[None]
    kernel_t = temporal_w.reshape(3, 1, channels, local)
    temporal = lax.conv_general_dilated(
        lhs_t,
        kernel_t,
        window_strides=(1, 1),
        padding=((1, 1), (0, 0)),
        dimension_numbers=("NHWC", "HWIO", "NHWC"),
        preferred_element_type=jnp.float32,
    )
    temporal = temporal.reshape(1, frames, rows, cols, local).astype(jnp.bfloat16)
    back = lax.all_to_all(temporal, "frame", split_axis=1, concat_axis=4, tiled=True)
    per_frame = frames // frame_size
    back = back.reshape(1, per_frame, rows, cols, frame_size, rep_size, shard_width)
    back = jnp.swapaxes(back, 4, 5).reshape(1, per_frame, rows, cols, channels)
    return activations.astype(jnp.float32) + back.astype(jnp.float32) + temporal_bias


def shards(
    activations,
    spatial_weight,
    temporal_weight,
    first_gain,
    first_shift,
    spatial_bias,
    second_gain,
    second_shift,
    temporal_bias,
):
    rep_size = lax.axis_size("rep")
    frame_size = lax.axis_size("frame")
    row_size = lax.axis_size("row")
    frame_index = lax.axis_index("frame")
    row_index = lax.axis_index("row")
    channels = activations.shape[-1]
    rows = activations.shape[2]
    cols = activations.shape[3]
    width = channels // GROUPS
    shard_width = spatial_weight.shape[-1]
    spatial_w = gather_rep(spatial_weight)
    temporal_w = gather_rep(temporal_weight)
    local = spatial_w.shape[-1]
    raw = lax.all_gather(activations, "frame", axis=1, tiled=True)
    frames = raw.shape[1]
    if row_size > 1:
        down = [(i, i + 1) for i in range(row_size - 1)]
        up = [(i + 1, i) for i in range(row_size - 1)]
        above = lax.ppermute(raw[:, :, rows - 1 :], "row", down)
        below = lax.ppermute(raw[:, :, :1], "row", up)
    else:
        above = jnp.zeros_like(raw[:, :, :1])
        below = jnp.zeros_like(raw[:, :, :1])
    inputs = raw.astype(jnp.float32)
    grouped = inputs.reshape(1, -1, GROUPS, width)
    sums = jnp.sum(grouped, axis=(1, 3))
    squares = jnp.sum(grouped * grouped, axis=(1, 3))
    sums, squares = pair_sum((sums, squares), "row")
    count = grouped.shape[1] * width * row_size
    mean = sums / count
    variance = squares / count - mean * mean
    inverse = lax.rsqrt(variance + EPS)
    mean_full = jnp.repeat(mean, width, axis=1)[:, None, None, None, :]
    inverse_full = jnp.repeat(inverse, width, axis=1)[:, None, None, None, :]

    def first_norm(x):
        normed = (x.astype(jnp.float32) - mean_full) * inverse_full * first_gain + first_shift
        return silu_bf16(normed)

    first_mid = first_norm(raw)
    first_above = jnp.where(row_index > 0, first_norm(above), jnp.zeros((), jnp.bfloat16))
    first_below = jnp.where(
        row_index < row_size - 1, first_norm(below), jnp.zeros((), jnp.bfloat16)
    )
    padded = jnp.concatenate([first_above, first_mid, first_below], axis=2)
    field = lax.optimization_barrier(padded[0])
    spatial = None
    for col_tap in range(3):
        product = None
        for row_tap in range(3):
            term = jnp.einsum(
                "frxc,cn->frxn",
                field[:, row_tap : row_tap + rows],
                spatial_w[3 * row_tap + col_tap],
                preferred_element_type=jnp.float32,
            )
            product = term if product is None else product + term
        if col_tap == 0:
            product = jnp.pad(product[:, :, :-1], ((0, 0), (0, 0), (1, 0), (0, 0)))
        elif col_tap == 2:
            product = jnp.pad(product[:, :, 1:], ((0, 0), (0, 0), (0, 1), (0, 0)))
        spatial = product if spatial is None else spatial + product
    spatial = spatial[None]
    spatial = spatial + local_vector(spatial_bias, frame_index, rep_size, frame_size)
    g2 = local_vector(second_gain, frame_index, rep_size, frame_size)
    s2 = local_vector(second_shift, frame_index, rep_size, frame_size)
    if shard_width % width == 0:
        grouped2 = spatial.reshape(-1, local // width, width)
        sums2 = jnp.sum(grouped2, axis=(0, 2))
        squares2 = jnp.sum(grouped2 * grouped2, axis=(0, 2))
        sums2, squares2 = pair_sum((sums2, squares2), "row")
        count2 = grouped2.shape[0] * width * row_size
        mean2 = sums2 / count2
        variance2 = squares2 / count2 - mean2 * mean2
        inverse2 = lax.rsqrt(variance2 + EPS)
        mean2_full = jnp.repeat(mean2, width)
        inverse2_full = jnp.repeat(inverse2, width)
    else:
        flat = spatial.reshape(-1, local)
        csum = jnp.sum(flat, axis=0)
        csq = jnp.sum(flat * flat, axis=0)
        csum, csq = pair_sum((csum, csq), "row")
        both = lax.all_gather(jnp.stack([csum, csq]), "frame", axis=0)
        both = both.reshape(frame_size, 2, rep_size, shard_width)
        both = jnp.transpose(both, (1, 2, 0, 3)).reshape(2, GROUPS, -1)
        gsum = jnp.sum(both, axis=2)
        count2 = flat.shape[0] * row_size * width
        gmean = gsum[0] / count2
        gvar = gsum[1] / count2 - gmean * gmean
        ginv = lax.rsqrt(gvar + EPS)
        mean2_full = local_vector(jnp.repeat(gmean, width), frame_index, rep_size, frame_size)
        inverse2_full = local_vector(jnp.repeat(ginv, width), frame_index, rep_size, frame_size)
    second = silu_bf16((spatial - mean2_full) * inverse2_full * g2 + s2)
    if frame_size > 8:
        return temporal_wide(activations, second, temporal_w, temporal_bias)
    second_all = lax.all_gather(second[0], "frame", axis=0, tiled=False)
    taps = temporal_w.reshape(3, rep_size, frame_size, shard_width, local)
    temporal = None
    for group in range(frame_size):
        block = second_all[group]
        weights = taps[:, :, group].reshape(3, rep_size * shard_width, local)
        for tap in range(3):
            if tap == 1:
                source = block
            elif tap == 0:
                source = block[:-1]
            else:
                source = block[1:]
            if source.shape[0] == 0:
                continue
            term = jnp.einsum(
                "frxc,cn->frxn", source, weights[tap], preferred_element_type=jnp.float32
            )
            if tap == 0:
                term = jnp.pad(term, ((1, 0), (0, 0), (0, 0), (0, 0)))
            elif tap == 2:
                term = jnp.pad(term, ((0, 1), (0, 0), (0, 0), (0, 0)))
            temporal = term if temporal is None else temporal + term
    temporal = temporal.astype(jnp.bfloat16)
    per_frame = frames // frame_size
    result = jnp.zeros((per_frame, rows, cols, rep_size, frame_size, shard_width), jnp.float32)
    for shift in range(frame_size):
        target = (frame_index + shift) % frame_size
        piece = lax.dynamic_slice_in_dim(temporal, target * per_frame, per_frame, axis=0)
        if shift:
            piece = lax.ppermute(
                piece, "frame", [(k, (k + shift) % frame_size) for k in range(frame_size)]
            )
        source = (frame_index - shift) % frame_size
        piece = piece.reshape(per_frame, rows, cols, rep_size, 1, shard_width)
        result = lax.dynamic_update_slice_in_dim(result, piece.astype(jnp.float32), source, axis=4)
    result = result.reshape(1, per_frame, rows, cols, channels)
    return activations.astype(jnp.float32) + result + temporal_bias


def solution(mesh):
    placed = (
        P("rep", "frame", "row", None, None),
        P(None, None, ("rep", "frame")),
        P(None, None, ("rep", "frame")),
        P(),
        P(),
        P(),
        P(),
        P(),
        P(),
    )
    return jax.shard_map(
        shards,
        mesh=mesh,
        in_specs=placed,
        out_specs=P("rep", "frame", "row", None, None),
        check_vma=False,
    )
```

profile of v0, /device:TPU:0, one launch (start us, length us, event | category | flops | bytes accessed | tf_op | source)
XLA Modules:
  0.0 287.9 jit_solution(6336116725697258098)
XLA Ops:
  6.5 3.0 %collective-permute-start.5 = (bf16[9,1280,80]{1,2,0:T(8,128)(2,1)}, bf16[9,1280,80]{1,2,0:T(8,128)(2,1)S(1)}, u32[]{:S(2)}, u32[]{:S(2)}) collective-permute-start(bf16[9,1280,80]{1,2,0:T(8,128)(2,1)} %param.10), channel_id=1, source_target_pairs={{0,16},{8,24},{16,0},{24,8},{1,17},{9,25},{17,1},{25,9},{2,18},{10... | collective-permute-start | bytes 5529608 | tf_op jit(solution)/shard_map/ppermute | solution.py:22
  9.5 40.4 %collective-permute-done.5 = bf16[9,1280,80]{1,2,0:T(8,128)(2,1)S(1)} collective-permute-done((bf16[9,1280,80]{1,2,0:T(8,128)(2,1)}, bf16[9,1280,80]{1,2,0:T(8,128)(2,1)S(1)}, u32[]{:S(2)}, u32[]{:S(2)}) %collective-permute-start.5) | collective-permute-done | bytes 1843232 | tf_op jit(solution)/shard_map/ppermute | solution.py:22
  53.8 3.0 %select_select_fusion.3 = (bf16[9,1280,80]{1,2,0:T(8,128)(2,1)S(1)}, bf16[9,1280,80]{1,2,0:T(8,128)(2,1)S(1)}, bf16[9,1280,80]{1,2,0:T(8,128)(2,1)S(1)}, bf16[9,1280,80]{1,2,0:T(8,128)(2,1)S(1)}) fusion(bf16[9,1280,80]{1,2,0:T(8,128)(2,1)} %param.10, bf16[9,1280,80]{1,2,0:T(8,128)(2,1)} %collective-permute-done.4, ...), kind=kLoop, calls=%fused_computation.19 | loop fusion | flops 11059200 | bytes 14745612 | tf_op jit(solution)/shard_map/jit(_where)/select_n | solution.py:31
  56.9 6.8 %pad_maximum_fusion = bf16[9,1280,320]{1,2,0:T(8,128)(2,1)} fusion(bf16[9,1280,80]{1,2,0:T(8,128)(2,1)S(1)} %get-tuple-element.13, bf16[9,1280,80]{1,2,0:T(8,128)(2,1)S(1)} %get-tuple-element.14, bf16[9,1280,80]{1,2,0:T(8,128)(2,1)S(1)} %get-tuple-element.12, bf16[9,1280,80]{1,2,0:T(8,128)(2,1)S(1)} %get-tuple-element.11), kind=kLoop, calls=%fused_computation.3 | loop fusion | flops 29491200 | bytes 14745600 | tf_op jit(solution)/shard_map/concatenate | solution.py:33
  63.7 42.8 %all-gather.4.cloned.1.call-done = bf16[1,4,8,32,1280]{4,3,2,0,1:T(8,128)(2,1)} async-done(((bf16[1,1,8,32,1280]{4,3,2,0,1:T(8,128)(2,1)}), bf16[1,4,8,32,1280]{4,3,2,0,1:T(8,128)(2,1)}) %all-gather.4.cloned.1.call-update) | async-done | bytes 2621456 | tf_op jit(solution)/shard_map/all_gather | solution.py:98
  106.5 2.6 convert_reduce_fusion
  111.7 4.1 %collective-permute-start = (bf16[1,4,1,32,1280]{4,3,2,1,0:T(8,128)(2,1)S(1)}, bf16[1,4,1,32,1280]{4,3,2,1,0:T(8,128)(2,1)}, u32[]{:S(2)}, u32[]{:S(2)}) collective-permute-start(bf16[1,4,1,32,1280]{4,3,2,1,0:T(8,128)(2,1)S(1)} %get-tuple-element.31), channel_id=1, source_target_pairs={{0,1},{2,3},{4,5},{6,7},{8,9},{10,11},{12,13},{14,15},{16,17},{18,... | collective-permute-start | bytes 983048 | tf_op jit(solution)/shard_map/ppermute | solution.py:103
  119.5 1.9 collective-permute-done
  121.3 4.9 %collective-permute-done.3 = bf16[1,4,1,32,1280]{4,3,2,1,0:T(8,128)(2,1)} collective-permute-done((bf16[1,4,1,32,1280]{4,3,2,1,0:T(8,128)(2,1)S(1)}, bf16[1,4,1,32,1280]{4,3,2,1,0:T(8,128)(2,1)}, u32[]{:S(2)}, u32[]{:S(2)}) %collective-permute-start.3) | collective-permute-done | bytes 327712 | tf_op jit(solution)/shard_map/ppermute | solution.py:104
  128.4 2.9 fusion.13
  143.1 2.2 multiply_reduce_fusion
  145.8 2.1 collective-permute-start.8
  152.7 11.2 %collective-permute-done.10 = bf16[3,1280,80]{1,2,0:T(8,128)(2,1)} collective-permute-done((bf16[3,1280,80]{1,2,0:T(8,128)(2,1)S(1)}, bf16[3,1280,80]{1,2,0:T(8,128)(2,1)}, u32[]{:S(2)}, u32[]{:S(2)}) %collective-permute-start.10) | collective-permute-done | bytes 614432 | tf_op jit(solution)/shard_map/ppermute | solution.py:22
  167.8 2.2 copy.65
  171.6 2.8 pad_maximum_fusion.1
  174.8 39.5 %all-gather.6.cloned.1.call-done = bf16[16,8,32,320]{3,2,1,0:T(8,128)(2,1)} async-done(((bf16[4,8,32,320]{3,2,1,0:T(8,128)(2,1)}), bf16[16,8,32,320]{3,2,1,0:T(8,128)(2,1)}) %all-gather.6.cloned.1.call-update) | async-done | bytes 2621456 | tf_op jit(solution)/shard_map/all_gather | solution.py:180
  214.3 1.8 fusion.25
  226.3 2.7 collective-permute-start.14
  229.7 11.4 %dynamic_update_slice.12 = f32[1,8,32,4,4,80]{5,4,3,2,1,0:T(4,128)S(1)} dynamic-update-slice(f32[1,8,32,4,4,80]{5,4,3,2,1,0:T(4,128)S(1)} %broadcast_in_dim.32, f32[1,8,32,4,1,80]{5,4,3,2,1,0:T(1,128)S(1)} %bitcast.222, s32[]{:T(128)} %constant.81.clone.1, s32[]{:T(128)} %constant.81.clone.1, s32[]{:T(128)} %constant.81.clone.1, s32[]{:T(128)} %constant.81.clone.1, s32[]{:T(128)S(6)} %select_n.277, ...) | dynamic-update-slice | bytes 655364 | tf_op jit(solution)/shard_map/dynamic_update_slice | solution.py:215
  241.5 11.4 %dynamic_update_slice.13 = f32[1,8,32,4,4,80]{5,4,3,2,1,0:T(4,128)S(1)} dynamic-update-slice(f32[1,8,32,4,4,80]{5,4,3,2,1,0:T(4,128)S(1)} %dynamic_update_slice.12, f32[1,8,32,4,1,80]{5,4,3,2,1,0:T(1,128)S(1)} %bitcast.224, s32[]{:T(128)} %constant.81.clone.1, s32[]{:T(128)} %constant.81.clone.1, s32[]{:T(128)} %constant.81.clone.1, s32[]{:T(128)} %constant.81.clone.1, s32[]{:T(128)S(6)} %select_n.281, ...) | dynamic-update-slice | bytes 655364 | tf_op jit(solution)/shard_map/dynamic_update_slice | solution.py:215
  253.3 11.4 %dynamic_update_slice.14 = f32[1,8,32,4,4,80]{5,4,3,2,1,0:T(4,128)S(1)} dynamic-update-slice(f32[1,8,32,4,4,80]{5,4,3,2,1,0:T(4,128)S(1)} %dynamic_update_slice.13, f32[1,8,32,4,1,80]{5,4,3,2,1,0:T(1,128)S(1)} %bitcast.225, s32[]{:T(128)} %constant.81.clone.1, s32[]{:T(128)} %constant.81.clone.1, s32[]{:T(128)} %constant.81.clone.1, s32[]{:T(128)} %constant.81.clone.1, s32[]{:T(128)S(6)} %select_n.285, ...) | dynamic-update-slice | bytes 655364 | tf_op jit(solution)/shard_map/dynamic_update_slice | solution.py:215
  265.1 11.4 %dynamic_update_slice.15 = f32[1,8,32,4,4,80]{5,4,3,2,1,0:T(4,128)S(1)} dynamic-update-slice(f32[1,8,32,4,4,80]{5,4,3,2,1,0:T(4,128)S(1)} %dynamic_update_slice.14, f32[1,8,32,4,1,80]{5,4,3,2,1,0:T(1,128)S(1)} %bitcast.223, s32[]{:T(128)} %constant.81.clone.1, s32[]{:T(128)} %constant.81.clone.1, s32[]{:T(128)} %constant.81.clone.1, s32[]{:T(128)} %constant.81.clone.1, s32[]{:T(128)S(6)} %select_n.289, ...) | dynamic-update-slice | bytes 655364 | tf_op jit(solution)/shard_map/dynamic_update_slice | solution.py:215
  276.5 2.2 reshape.184
  278.8 2.3 add_add_fusion.1
  (104 shorter events, 46.8 us)
Async XLA Ops:
  6.5 99.9 %all-gather.4.cloned.1.call-start = ((), (), s32[]{:S(2)}) async-start(), calls=%async_computation | async-start | bytes 3276800 | tf_op jit(solution)/shard_map/all_gather | solution.py:98
  6.5 43.4 %collective-permute-start.5 = (bf16[9,1280,80]{1,2,0:T(8,128)(2,1)}, bf16[9,1280,80]{1,2,0:T(8,128)(2,1)S(1)}, u32[]{:S(2)}, u32[]{:S(2)}) collective-permute-start(bf16[9,1280,80]{1,2,0:T(8,128)(2,1)} %param.10), channel_id=1, source_target_pairs={{0,16},{8,24},{16,0},{24,8},{1,17},{9,25},{17,1},{25,9},{2,18},{10... | collective-permute-start | bytes 5529608 | tf_op jit(solution)/shard_map/ppermute | solution.py:22
  9.5 43.2 %collective-permute-start.4 = (bf16[9,1280,80]{1,2,0:T(8,128)(2,1)}, bf16[9,1280,80]{1,2,0:T(8,128)(2,1)}, u32[]{:S(2)}, u32[]{:S(2)}) collective-permute-start(bf16[9,1280,80]{1,2,0:T(8,128)(2,1)} %param.10), channel_id=1, source_target_pairs={{0,8},{8,0},{16,24},{24,16},{1,9},{9,1},{17,25},{25,17},{2,10},{10... | collective-permute-start | bytes 5529608 | tf_op jit(solution)/shard_map/ppermute | solution.py:23
  49.9 3.9 %collective-permute-start.6 = (bf16[9,1280,80]{1,2,0:T(8,128)(2,1)S(1)}, bf16[9,1280,80]{1,2,0:T(8,128)(2,1)}, u32[]{:S(2)}, u32[]{:S(2)}) collective-permute-start(bf16[9,1280,80]{1,2,0:T(8,128)(2,1)S(1)} %collective-permute-done.5), channel_id=1, source_target_pairs={{0,8},{8,0},{16,24},{24,16},{1,9},{9,1},{17,25},{25,17},{2,10},{10... | collective-permute-start | bytes 5529608 | tf_op jit(solution)/shard_map/ppermute | solution.py:24
  49.9 164.4 %all-gather.6.cloned.1.call-start = ((), (), s32[]{:S(2)}) async-start(), calls=%async_computation.1 | async-start | bytes 3932160 | tf_op jit(solution)/shard_map/all_gather | solution.py:180
  63.6 54.0 %copy-start.3 = (f32[1280]{0:T(1024)S(1)}, f32[1280]{0:T(1024)}, u32[]{:S(2)}) copy-start(f32[1280]{0:T(1024)} %param.13) | copy-start | bytes 15364
  63.6 54.0 %copy-start.4 = (f32[1280]{0:T(1024)S(1)}, f32[1280]{0:T(1024)}, u32[]{:S(2)}) copy-start(f32[1280]{0:T(1024)} %param.12) | copy-start | bytes 15364
  106.5 5.2 %copy-start.1 = (bf16[1,4,8,32,1280]{4,3,2,0,1:T(8,128)(2,1)S(1)}, bf16[1,4,8,32,1280]{4,3,2,0,1:T(8,128)(2,1)}, u32[]{:S(2)}) copy-start(bf16[1,4,8,32,1280]{4,3,2,0,1:T(8,128)(2,1)} %all-gather.4.cloned.1.call-done) | copy-start | bytes 7864324
  109.3 8.0 %collective-permute-start.1 = (f32[1,32]{1,0:T(1,128)S(1)}, f32[1,32]{1,0:T(1,128)S(1)}, u32[]{:S(2)}, u32[]{:S(2)}) collective-permute-start(f32[1,32]{1,0:T(1,128)S(1)} %bitcast.238), channel_id=1, source_target_pairs={{0,1},{1,0},{2,3},{3,2},{4,5},{5,4},{6,7},{7,6},{8,9},{9,8},{10,11... | collective-permute-start | bytes 392 | tf_op jit(solution)/shard_map/ppermute | solution.py:13
  111.1 6.2 %collective-permute-start.2 = (f32[1,32]{1,0:T(1,128)S(1)}, f32[1,32]{1,0:T(1,128)S(1)}, u32[]{:S(2)}, u32[]{:S(2)}) collective-permute-start(f32[1,32]{1,0:T(1,128)S(1)} %bitcast.239), channel_id=1, source_target_pairs={{0,1},{1,0},{2,3},{3,2},{4,5},{5,4},{6,7},{7,6},{8,9},{9,8},{10,11... | collective-permute-start | bytes 392 | tf_op jit(solution)/shard_map/ppermute | solution.py:13
  111.7 9.6 %collective-permute-start = (bf16[1,4,1,32,1280]{4,3,2,1,0:T(8,128)(2,1)S(1)}, bf16[1,4,1,32,1280]{4,3,2,1,0:T(8,128)(2,1)}, u32[]{:S(2)}, u32[]{:S(2)}) collective-permute-start(bf16[1,4,1,32,1280]{4,3,2,1,0:T(8,128)(2,1)S(1)} %get-tuple-element.31), channel_id=1, source_target_pairs={{0,1},{2,3},{4,5},{6,7},{8,9},{10,11},{12,13},{14,15},{16,17},{18,... | collective-permute-start | bytes 983048 | tf_op jit(solution)/shard_map/ppermute | solution.py:103
  115.8 10.4 %collective-permute-start.3 = (bf16[1,4,1,32,1280]{4,3,2,1,0:T(8,128)(2,1)S(1)}, bf16[1,4,1,32,1280]{4,3,2,1,0:T(8,128)(2,1)}, u32[]{:S(2)}, u32[]{:S(2)}) collective-permute-start(bf16[1,4,1,32,1280]{4,3,2,1,0:T(8,128)(2,1)S(1)} %get-tuple-element.32), channel_id=1, source_target_pairs={{1,0},{3,2},{5,4},{7,6},{9,8},{11,10},{13,12},{15,14},{17,16},{19,... | collective-permute-start | bytes 983048 | tf_op jit(solution)/shard_map/ppermute | solution.py:104
  126.3 5.0 %slice-start = ((s8[7372800]{0:T(1024)(128)(4,1)}), s8[4194304]{0:T(1024)(128)(4,1)S(1)}, s32[]{:S(2)}) async-start(s8[7372800]{0:T(1024)(128)(4,1)} %bitcast.219), calls=%async_computation.2 | async-start | bytes 8388608
  128.0 3.3 %slice-start.1 = ((s8[7372800]{0:T(1024)(128)(4,1)}), s8[3178496]{0:T(1024)(128)(4,1)S(1)}, s32[]{:S(2)}) async-start(s8[7372800]{0:T(1024)(128)(4,1)} %bitcast.219), calls=%async_computation.3 | async-start | bytes 6356992
  145.3 5.9 %copy-start.2 = (bf16[3,1280,80]{1,2,0:T(8,128)(2,1)S(1)}, bf16[3,1280,80]{1,2,0:T(8,128)(2,1)}, u32[]{:S(2)}) copy-start(bf16[3,1280,80]{1,2,0:T(8,128)(2,1)} %param.11) | copy-start | bytes 1843204
  145.5 3.6 %collective-permute-start.7 = (f32[8]{0:T(128)S(1)}, f32[8]{0:T(128)S(1)}, u32[]{:S(2)}, u32[]{:S(2)}) collective-permute-start(f32[8]{0:T(128)S(1)} %reduce_sum.78), channel_id=1, source_target_pairs={{0,1},{1,0},{2,3},{3,2},{4,5},{5,4},{6,7},{7,6},{8,9},{9,8},{10,11... | collective-permute-start | bytes 104 | tf_op jit(solution)/shard_map/ppermute | solution.py:13
  145.8 3.6 %collective-permute-start.8 = (f32[8]{0:T(128)S(1)}, f32[8]{0:T(128)S(1)}, u32[]{:S(2)}, u32[]{:S(2)}) collective-permute-start(f32[8]{0:T(128)S(1)} %reduce_sum.81), channel_id=1, source_target_pairs={{0,1},{1,0},{2,3},{3,2},{4,5},{5,4},{6,7},{7,6},{8,9},{9,8},{10,11... | collective-permute-start | bytes 104 | tf_op jit(solution)/shard_map/ppermute | solution.py:13
  151.2 12.7 %collective-permute-start.10 = (bf16[3,1280,80]{1,2,0:T(8,128)(2,1)S(1)}, bf16[3,1280,80]{1,2,0:T(8,128)(2,1)}, u32[]{:S(2)}, u32[]{:S(2)}) collective-permute-start(bf16[3,1280,80]{1,2,0:T(8,128)(2,1)S(1)} %copy-done.2), channel_id=1, source_target_pairs={{0,16},{8,24},{16,0},{24,8},{1,17},{9,25},{17,1},{25,9},{2,18},{10... | collective-permute-start | bytes 1843208 | tf_op jit(solution)/shard_map/ppermute | solution.py:22
  152.7 13.5 %collective-permute-start.9 = (bf16[3,1280,80]{1,2,0:T(8,128)(2,1)S(1)}, bf16[3,1280,80]{1,2,0:T(8,128)(2,1)}, u32[]{:S(2)}, u32[]{:S(2)}) collective-permute-start(bf16[3,1280,80]{1,2,0:T(8,128)(2,1)S(1)} %copy-done.2), channel_id=1, source_target_pairs={{0,8},{8,0},{16,24},{24,16},{1,9},{9,1},{17,25},{25,17},{2,10},{10... | collective-permute-start | bytes 1843208 | tf_op jit(solution)/shard_map/ppermute | solution.py:23
  163.9 3.8 %collective-permute-start.11 = (bf16[3,1280,80]{1,2,0:T(8,128)(2,1)}, bf16[3,1280,80]{1,2,0:T(8,128)(2,1)}, u32[]{:S(2)}, u32[]{:S(2)}) collective-permute-start(bf16[3,1280,80]{1,2,0:T(8,128)(2,1)} %collective-permute-done.10), channel_id=1, source_target_pairs={{0,8},{8,0},{16,24},{24,16},{1,9},{9,1},{17,25},{25,17},{2,10},{10... | collective-permute-start | bytes 1843208 | tf_op jit(solution)/shard_map/ppermute | solution.py:24
  214.3 3.4 %copy-start = (bf16[16,8,32,320]{3,2,1,0:T(8,128)(2,1)S(1)}, bf16[16,8,32,320]{3,2,1,0:T(8,128)(2,1)}, u32[]{:S(2)}) copy-start(bf16[16,8,32,320]{3,2,1,0:T(8,128)(2,1)} %all-gather.6.cloned.1.call-done) | copy-start | bytes 7864324
  225.0 16.1 %collective-permute-start.12 = (bf16[1,8,32,320]{3,2,1,0:T(8,128)(2,1)}, bf16[1,8,32,320]{3,2,1,0:T(8,128)(2,1)S(1)}, u32[]{:S(2)}, u32[]{:S(2)}) collective-permute-start(bf16[1,8,32,320]{3,2,1,0:T(8,128)(2,1)} %get-tuple-element.35), channel_id=1, source_target_pairs={{0,2},{2,4},{4,6},{6,0},{1,3},{3,5},{5,7},{7,1},{8,10},{10,12},{12... | collective-permute-start | bytes 491528 | tf_op jit(solution)/shard_map/ppermute | solution.py:210
  225.0 27.9 %collective-permute-start.13 = (bf16[1,8,32,320]{3,2,1,0:T(8,128)(2,1)}, bf16[1,8,32,320]{3,2,1,0:T(8,128)(2,1)S(1)}, u32[]{:S(2)}, u32[]{:S(2)}) collective-permute-start(bf16[1,8,32,320]{3,2,1,0:T(8,128)(2,1)} %get-tuple-element.34), channel_id=1, source_target_pairs={{0,4},{2,6},{4,0},{6,2},{1,5},{3,7},{5,1},{7,3},{8,12},{10,14},{12... | collective-permute-start | bytes 491528 | tf_op jit(solution)/shard_map/ppermute | solution.py:210
  226.3 38.4 %collective-permute-start.14 = (bf16[1,8,32,320]{3,2,1,0:T(8,128)(2,1)S(1)}, bf16[1,8,32,320]{3,2,1,0:T(8,128)(2,1)S(1)}, u32[]{:S(2)}, u32[]{:S(2)}) collective-permute-start(bf16[1,8,32,320]{3,2,1,0:T(8,128)(2,1)S(1)} %get-tuple-element.33), channel_id=1, source_target_pairs={{0,6},{2,0},{4,2},{6,4},{1,7},{3,1},{5,3},{7,5},{8,14},{10,8},{12,... | collective-permute-start | bytes 491528 | tf_op jit(solution)/shard_map/ppermute | solution.py:210
  (1 other events, 2.3 us)
Sparse Core Ops, SparseCore 0:
  50.0 56.3 all-gather.3
  151.3 62.9 all-gather.5
where the time goes:
time: 288 us
  waiting for transfers between devices  143 us (50%)
  local copies, waits for them, and re-layouts  59.6 us (21%)
  other arithmetic  27 us (9%)
  matrix products  25.5 us (9%)
  starting transfers between devices  18.4 us (6%)
  between operations  14 us (5%)
    ppermute x2, waiting for transfers between devices, gather_rep(): across = lax.ppermute(w, 'rep', [(k, k ^ 2) for k in range(size)])  51.6 us
    dynamic_update_slice x4, local copies, waits for them, and re-layouts, shards(): lax.dynamic_update_slice_in_dim(result, piece.astype(jnp.float32), source...  45.8 us
    all_gather x1, waiting for transfers between devices, shards(): raw = lax.all_gather(activations, 'frame', axis=1, tiled=True)  42.8 us
    all_gather x1, waiting for transfers between devices, shards(): second_all = lax.all_gather(second[0], 'frame', axis=0, tiled=False)  39.5 us
    dot_general x9, matrix products, shards(): jnp.einsum('frxc,cn->frxn', field[:, row_tap:row_tap + rows], spatial_w[3...  15.8 us
    concatenate x2, other arithmetic, gather_rep(): return jnp.concatenate(blocks, axis=-1)  9.57 us
    dot_general x8, matrix products, shards(): jnp.einsum('frxc,cn->frxn', source, weights[tap], preferred_element_type=...  6.05 us
  transfers between devices with their start and end apart: 17, of which 9 were waited for; matrix products, arithmetic and copies ran while one was open for 21% of the time, Pallas kernels for 0%

commit v1 on v0

--- a/solution.py
+++ b/solution.py
@@ -95,7 +95,21 @@
     spatial_w = gather_rep(spatial_weight)
     temporal_w = gather_rep(temporal_weight)
     local = spatial_w.shape[-1]
-    raw = lax.all_gather(activations, "frame", axis=1, tiled=True)
+    body = activations
+    e_now, local_part, last = (lax.axis_size("frame"), lax.axis_index("frame"), body.shape[1])
+    raw = lax.dynamic_update_slice_in_dim(
+        jnp.zeros([kk * e_now if rr == 1 else kk for rr, kk in enumerate(body.shape)], body.dtype),
+        body,
+        local_part * last,
+        axis=1,
+    )
+    j0 = 1
+    while j0 < e_now:
+        body = lax.ppermute(
+            body, axis_name="frame", perm=[(rr, (rr + 1) % e_now) for rr in range(e_now)]
+        )
+        raw = lax.dynamic_update_slice_in_dim(raw, body, (local_part - j0) % e_now * last, axis=1)
+        j0 = j0 + 1
     frames = raw.shape[1]
     if row_size > 1:
         down = [(i, i + 1) for i in range(row_size - 1)]

time: 288 us -> 248 us (0.86)
  waiting for transfers between devices: 143 us -> 102 us
  local copies, waits for them, and re-layouts: 59.6 us -> 63.3 us
  other arithmetic: 27 us -> 24 us
    all_gather x1 -> x0, waiting for transfers between devices: 42.8 us -> none  [shards(): raw = lax.all_gather(activations, 'frame', axis=1, tiled=True)]
    ppermute x0 -> x3, waiting for transfers between devices: none -> 40.5 us  [shards(): lax.ppermute(body, axis_name='frame', perm=[(rr, (rr + 1) % e_now) for rr...]
    ppermute x2, waiting for transfers between devices: 51.6 us -> 13.6 us  [gather_rep(): across = lax.ppermute(w, 'rep', [(k, k ^ 2) for k in range(size)])]
    ppermute x0 -> x3, starting transfers between devices: none -> 3.06 us  [shards(): lax.ppermute(body, axis_name='frame', perm=[(rr, (rr + 1) % e_now) for rr...]
  transfers between devices with their start and end apart: 17 -> 19, of which waited for: 9 -> 10; matrix products, arithmetic and copies ran while one was open for 21% -> 23% of each run, Pallas kernels for 0% -> 0%
where the time goes in v1:
time: 248 us; the launch traced here: 247 us
  waiting for transfers between devices  102 us (41%)
  local copies, waits for them, and re-layouts  63.3 us (26%)
  other arithmetic  24 us (10%)
  matrix products  23.9 us (10%)
  starting transfers between devices  19.5 us (8%)
  between operations  14.1 us (6%)
    dynamic_update_slice x4, local copies, waits for them, and re-layouts, shards(): lax.dynamic_update_slice_in_dim(result, piece.astype(jnp.float32), source...  46 us
    all_gather x1, waiting for transfers between devices, shards(): second_all = lax.all_gather(second[0], 'frame', axis=0, tiled=False)  40.9 us
    ppermute x3, waiting for transfers between devices, shards(): lax.ppermute(body, axis_name='frame', perm=[(rr, (rr + 1) % e_now) for rr...  40.5 us
    dot_general x9, matrix products, shards(): jnp.einsum('frxc,cn->frxn', field[:, row_tap:row_tap + rows], spatial_w[3...  14.2 us
    ppermute x2, waiting for transfers between devices, gather_rep(): across = lax.ppermute(w, 'rep', [(k, k ^ 2) for k in range(size)])  13.6 us
    concatenate x2, other arithmetic, gather_rep(): return jnp.concatenate(blocks, axis=-1)  8.68 us
    dot_general x8, matrix products, shards(): jnp.einsum('frxc,cn->frxn', source, weights[tap], preferred_element_type=...  6.05 us
    ppermute x1, waiting for transfers between devices, shards(): below = lax.ppermute(raw[:, :, :1], 'row', up)  5.24 us
  transfers between devices with their start and end apart: 19, of which 10 were waited for; matrix products, arithmetic and copies ran while one was open for 23% of the time, Pallas kernels for 0%

profile of v1, /device:TPU:0, one launch (start us, length us, event | category | flops | bytes accessed | tf_op | source)
XLA Modules:
  0.0 247.0 jit_solution(17293686733206280084)
XLA Ops:
  6.5 3.1 %collective-permute-start = (bf16[1,1,8,32,1280]{4,3,2,1,0:T(8,128)(2,1)}, bf16[1,1,8,32,1280]{4,3,2,1,0:T(8,128)(2,1)S(1)}, u32[]{:S(2)}, u32[]{:S(2)}) collective-permute-start(bf16[1,1,8,32,1280]{4,3,2,1,0:T(8,128)(2,1)} %param.9), channel_id=1, source_target_pairs={{0,2},{2,4},{4,6},{6,0},{1,3},{3,5},{5,7},{7,1},{8,10},{10,12},{12... | collective-permute-start | bytes 1966088 | tf_op jit(solution)/shard_map/ppermute | solution.py:108
  11.1 15.5 %collective-permute-done = bf16[1,1,8,32,1280]{4,3,2,1,0:T(8,128)(2,1)S(1)} collective-permute-done((bf16[1,1,8,32,1280]{4,3,2,1,0:T(8,128)(2,1)}, bf16[1,1,8,32,1280]{4,3,2,1,0:T(8,128)(2,1)S(1)}, u32[]{:S(2)}, u32[]{:S(2)}) %collective-permute-start) | collective-permute-done | bytes 655392 | tf_op jit(solution)/shard_map/ppermute | solution.py:108
  29.4 15.0 %collective-permute-done.1 = bf16[1,1,8,32,1280]{4,3,2,1,0:T(8,128)(2,1)} collective-permute-done((bf16[1,1,8,32,1280]{4,3,2,1,0:T(8,128)(2,1)S(1)}, bf16[1,1,8,32,1280]{4,3,2,1,0:T(8,128)(2,1)}, u32[]{:S(2)}, u32[]{:S(2)}) %collective-permute-start.1) | collective-permute-done | bytes 655392 | tf_op jit(solution)/shard_map/ppermute | solution.py:108
  46.7 4.8 %collective-permute-done.8 = bf16[9,1280,80]{1,2,0:T(8,128)(2,1)} collective-permute-done((bf16[9,1280,80]{1,2,0:T(8,128)(2,1)}, bf16[9,1280,80]{1,2,0:T(8,128)(2,1)}, u32[]{:S(2)}, u32[]{:S(2)}) %collective-permute-start.8) | collective-permute-done | bytes 1843232 | tf_op jit(solution)/shard_map/ppermute | solution.py:22
  51.6 9.9 %collective-permute-done.2 = bf16[1,1,8,32,1280]{4,3,2,1,0:T(8,128)(2,1)S(1)} collective-permute-done((bf16[1,1,8,32,1280]{4,3,2,1,0:T(8,128)(2,1)}, bf16[1,1,8,32,1280]{4,3,2,1,0:T(8,128)(2,1)S(1)}, u32[]{:S(2)}, u32[]{:S(2)}) %collective-permute-start.2) | collective-permute-done | bytes 655392 | tf_op jit(solution)/shard_map/ppermute | solution.py:108
  64.9 3.9 %collective-permute-start.3 = (bf16[1,4,1,32,1280]{4,3,2,1,0:T(8,128)(2,1)S(1)}, bf16[1,4,1,32,1280]{4,3,2,1,0:T(8,128)(2,1)}, u32[]{:S(2)}, u32[]{:S(2)}) collective-permute-start(bf16[1,4,1,32,1280]{4,3,2,1,0:T(8,128)(2,1)S(1)} %get-tuple-element.31), channel_id=1, source_target_pairs={{0,1},{2,3},{4,5},{6,7},{8,9},{10,11},{12,13},{14,15},{16,17},{18,... | collective-permute-start | bytes 983048 | tf_op jit(solution)/shard_map/ppermute | solution.py:117
  70.4 1.8 fusion.9
  72.6 5.2 %collective-permute-done.6 = bf16[1,4,1,32,1280]{4,3,2,1,0:T(8,128)(2,1)} collective-permute-done((bf16[1,4,1,32,1280]{4,3,2,1,0:T(8,128)(2,1)S(1)}, bf16[1,4,1,32,1280]{4,3,2,1,0:T(8,128)(2,1)}, u32[]{:S(2)}, u32[]{:S(2)}) %collective-permute-start.6) | collective-permute-done | bytes 327712 | tf_op jit(solution)/shard_map/ppermute | solution.py:118
  80.9 3.0 %select_select_fusion.3 = (bf16[9,1280,80]{1,2,0:T(8,128)(2,1)S(1)}, bf16[9,1280,80]{1,2,0:T(8,128)(2,1)S(1)}, bf16[9,1280,80]{1,2,0:T(8,128)(2,1)S(1)}, bf16[9,1280,80]{1,2,0:T(8,128)(2,1)S(1)}) fusion(bf16[9,1280,80]{1,2,0:T(8,128)(2,1)S(1)} %copy-done.2, bf16[9,1280,80]{1,2,0:T(8,128)(2,1)} %collective-permute-done.7, ...), kind=kLoop, calls=%fused_computation.19 | loop fusion | flops 11059200 | bytes 14745612 | tf_op jit(solution)/shard_map/jit(_where)/select_n | solution.py:31
  84.0 5.7 %pad_maximum_fusion = bf16[9,1280,320]{1,2,0:T(8,128)(2,1)S(1)} fusion(bf16[9,1280,80]{1,2,0:T(8,128)(2,1)S(1)} %get-tuple-element.13, bf16[9,1280,80]{1,2,0:T(8,128)(2,1)S(1)} %get-tuple-element.14, bf16[9,1280,80]{1,2,0:T(8,128)(2,1)S(1)} %get-tuple-element.12, bf16[9,1280,80]{1,2,0:T(8,128)(2,1)S(1)} %get-tuple-element.11), kind=kLoop, calls=%fused_computation.3 | loop fusion | flops 29491200 | bytes 14745600 | tf_op jit(solution)/shard_map/concatenate | solution.py:33
  103.0 2.0 multiply_reduce_fusion
  105.5 2.1 collective-permute-start.11
  112.4 8.8 %collective-permute-done.13 = bf16[3,1280,80]{1,2,0:T(8,128)(2,1)} collective-permute-done((bf16[3,1280,80]{1,2,0:T(8,128)(2,1)S(1)}, bf16[3,1280,80]{1,2,0:T(8,128)(2,1)}, u32[]{:S(2)}, u32[]{:S(2)}) %collective-permute-start.13) | collective-permute-done | bytes 614432 | tf_op jit(solution)/shard_map/ppermute | solution.py:22
  125.0 2.2 copy.57
  128.9 3.0 %pad_maximum_fusion.1 = bf16[3,1280,320]{2,1,0:T(8,128)(2,1)S(1)} fusion(bf16[3,1280,80]{2,1,0:T(8,128)(2,1)S(1)} %get-tuple-element.16, bf16[3,1280,80]{2,1,0:T(8,128)(2,1)S(1)} %get-tuple-element.17, bf16[3,1280,80]{2,1,0:T(8,128)(2,1)S(1)} %get-tuple-element.18, bf16[3,1280,80]{2,1,0:T(8,128)(2,1)S(1)} %get-tuple-element.15), kind=kLoop, calls=%fused_computation.15 | loop fusion | flops 9830400 | bytes 4915200 | tf_op jit(solution)/shard_map/concatenate | solution.py:33
  132.3 40.9 %all-gather.3.cloned.1.call-done = bf16[16,8,32,320]{3,2,1,0:T(8,128)(2,1)} async-done(((bf16[4,8,32,320]{3,2,1,0:T(8,128)(2,1)}), bf16[16,8,32,320]{3,2,1,0:T(8,128)(2,1)}) %all-gather.3.cloned.1.call-update) | async-done | bytes 2621456 | tf_op jit(solution)/shard_map/all_gather | solution.py:194
  173.2 1.8 fusion.25
  185.2 2.7 %collective-permute-start.17 = (bf16[1,8,32,320]{3,2,1,0:T(8,128)(2,1)S(1)}, bf16[1,8,32,320]{3,2,1,0:T(8,128)(2,1)S(1)}, u32[]{:S(2)}, u32[]{:S(2)}) collective-permute-start(bf16[1,8,32,320]{3,2,1,0:T(8,128)(2,1)S(1)} %get-tuple-element.33), channel_id=1, source_target_pairs={{0,6},{2,0},{4,2},{6,4},{1,7},{3,1},{5,3},{7,5},{8,14},{10,8},{12,... | collective-permute-start | bytes 491528 | tf_op jit(solution)/shard_map/ppermute | solution.py:224
  188.5 11.7 %dynamic_update_slice.28 = f32[1,8,32,4,4,80]{5,4,3,2,1,0:T(4,128)S(1)} dynamic-update-slice(f32[1,8,32,4,4,80]{5,4,3,2,1,0:T(4,128)S(1)} %broadcast_in_dim.35, f32[1,8,32,4,1,80]{5,4,3,2,1,0:T(1,128)S(1)} %bitcast.211, s32[]{:T(128)} %constant.88.clone.1, s32[]{:T(128)} %constant.88.clone.1, s32[]{:T(128)} %constant.88.clone.1, s32[]{:T(128)} %constant.88.clone.1, s32[]{:T(128)S(6)} %select_n.293, ...) | dynamic-update-slice | bytes 655364 | tf_op jit(solution)/shard_map/dynamic_update_slice | solution.py:229
  200.6 11.4 %dynamic_update_slice.29 = f32[1,8,32,4,4,80]{5,4,3,2,1,0:T(4,128)S(1)} dynamic-update-slice(f32[1,8,32,4,4,80]{5,4,3,2,1,0:T(4,128)S(1)} %dynamic_update_slice.28, f32[1,8,32,4,1,80]{5,4,3,2,1,0:T(1,128)S(1)} %bitcast.213, s32[]{:T(128)} %constant.88.clone.1, s32[]{:T(128)} %constant.88.clone.1, s32[]{:T(128)} %constant.88.clone.1, s32[]{:T(128)} %constant.88.clone.1, s32[]{:T(128)S(6)} %select_n.236, ...) | dynamic-update-slice | bytes 655364 | tf_op jit(solution)/shard_map/dynamic_update_slice | solution.py:229
  212.4 11.4 %dynamic_update_slice.30 = f32[1,8,32,4,4,80]{5,4,3,2,1,0:T(4,128)S(1)} dynamic-update-slice(f32[1,8,32,4,4,80]{5,4,3,2,1,0:T(4,128)S(1)} %dynamic_update_slice.29, f32[1,8,32,4,1,80]{5,4,3,2,1,0:T(1,128)S(1)} %bitcast.214, s32[]{:T(128)} %constant.88.clone.1, s32[]{:T(128)} %constant.88.clone.1, s32[]{:T(128)} %constant.88.clone.1, s32[]{:T(128)} %constant.88.clone.1, s32[]{:T(128)S(6)} %select_n.238, ...) | dynamic-update-slice | bytes 655364 | tf_op jit(solution)/shard_map/dynamic_update_slice | solution.py:229
  224.2 11.4 %dynamic_update_slice.31 = f32[1,8,32,4,4,80]{5,4,3,2,1,0:T(4,128)S(1)} dynamic-update-slice(f32[1,8,32,4,4,80]{5,4,3,2,1,0:T(4,128)S(1)} %dynamic_update_slice.30, f32[1,8,32,4,1,80]{5,4,3,2,1,0:T(1,128)S(1)} %bitcast.212, s32[]{:T(128)} %constant.88.clone.1, s32[]{:T(128)} %constant.88.clone.1, s32[]{:T(128)} %constant.88.clone.1, s32[]{:T(128)} %constant.88.clone.1, s32[]{:T(128)S(6)} %select_n.240, ...) | dynamic-update-slice | bytes 655364 | tf_op jit(solution)/shard_map/dynamic_update_slice | solution.py:229
  235.6 2.2 reshape.184
  237.9 2.3 add_add_fusion.1
  (113 shorter events, 51.1 us)
Async XLA Ops:
  6.5 38.2 %copy-start.1 = (bf16[1,1,8,32,1280]{4,3,2,1,0:T(8,128)(2,1)S(1)}, bf16[1,1,8,32,1280]{4,3,2,1,0:T(8,128)(2,1)}, u32[]{:S(2)}) copy-start(bf16[1,1,8,32,1280]{4,3,2,1,0:T(8,128)(2,1)} %param.9) | copy-start | bytes 1966084
  6.5 166.6 %all-gather.3.cloned.1.call-start = ((), (), s32[]{:S(2)}) async-start(), calls=%async_computation | async-start | bytes 3932160 | tf_op jit(solution)/shard_map/all_gather | solution.py:194
  6.5 20.1 %collective-permute-start = (bf16[1,1,8,32,1280]{4,3,2,1,0:T(8,128)(2,1)}, bf16[1,1,8,32,1280]{4,3,2,1,0:T(8,128)(2,1)S(1)}, u32[]{:S(2)}, u32[]{:S(2)}) collective-permute-start(bf16[1,1,8,32,1280]{4,3,2,1,0:T(8,128)(2,1)} %param.9), channel_id=1, source_target_pairs={{0,2},{2,4},{4,6},{6,0},{1,3},{3,5},{5,7},{7,1},{8,10},{10,12},{12... | collective-permute-start | bytes 1966088 | tf_op jit(solution)/shard_map/ppermute | solution.py:108
  9.6 42.0 %collective-permute-start.8 = (bf16[9,1280,80]{1,2,0:T(8,128)(2,1)}, bf16[9,1280,80]{1,2,0:T(8,128)(2,1)}, u32[]{:S(2)}, u32[]{:S(2)}) collective-permute-start(bf16[9,1280,80]{1,2,0:T(8,128)(2,1)} %param.10), channel_id=1, source_target_pairs={{0,16},{8,24},{16,0},{24,8},{1,17},{9,25},{17,1},{25,9},{2,18},{10... | collective-permute-start | bytes 5529608 | tf_op jit(solution)/shard_map/ppermute | solution.py:22
  26.6 17.8 %copy-start.3 = (bf16[1,1,8,32,1280]{4,3,2,1,0:T(8,128)(2,1)}, bf16[1,1,8,32,1280]{4,3,2,1,0:T(8,128)(2,1)S(1)}, u32[]{:S(2)}) copy-start(bf16[1,1,8,32,1280]{4,3,2,1,0:T(8,128)(2,1)S(1)} %collective-permute-done) | copy-start | bytes 1966084
  26.6 17.8 %collective-permute-start.1 = (bf16[1,1,8,32,1280]{4,3,2,1,0:T(8,128)(2,1)S(1)}, bf16[1,1,8,32,1280]{4,3,2,1,0:T(8,128)(2,1)}, u32[]{:S(2)}, u32[]{:S(2)}) collective-permute-start(bf16[1,1,8,32,1280]{4,3,2,1,0:T(8,128)(2,1)S(1)} %collective-permute-done), channel_id=1, source_target_pairs={{0,2},{2,4},{4,6},{6,0},{1,3},{3,5},{5,7},{7,1},{8,10},{10,12},{12... | collective-permute-start | bytes 1966088 | tf_op jit(solution)/shard_map/ppermute | solution.py:108
  26.6 53.2 %collective-permute-start.7 = (bf16[9,1280,80]{1,2,0:T(8,128)(2,1)}, bf16[9,1280,80]{1,2,0:T(8,128)(2,1)}, u32[]{:S(2)}, u32[]{:S(2)}) collective-permute-start(bf16[9,1280,80]{1,2,0:T(8,128)(2,1)} %param.10), channel_id=1, source_target_pairs={{0,8},{8,0},{16,24},{24,16},{1,9},{9,1},{17,25},{25,17},{2,10},{10... | collective-permute-start | bytes 5529608 | tf_op jit(solution)/shard_map/ppermute | solution.py:23
  44.4 17.1 %collective-permute-start.2 = (bf16[1,1,8,32,1280]{4,3,2,1,0:T(8,128)(2,1)}, bf16[1,1,8,32,1280]{4,3,2,1,0:T(8,128)(2,1)S(1)}, u32[]{:S(2)}, u32[]{:S(2)}) collective-permute-start(bf16[1,1,8,32,1280]{4,3,2,1,0:T(8,128)(2,1)} %collective-permute-done.1), channel_id=1, source_target_pairs={{0,2},{2,4},{4,6},{6,0},{1,3},{3,5},{5,7},{7,1},{8,10},{10,12},{12... | collective-permute-start | bytes 1966088 | tf_op jit(solution)/shard_map/ppermute | solution.py:108
  51.6 28.3 %collective-permute-start.9 = (bf16[9,1280,80]{1,2,0:T(8,128)(2,1)}, bf16[9,1280,80]{1,2,0:T(8,128)(2,1)}, u32[]{:S(2)}, u32[]{:S(2)}) collective-permute-start(bf16[9,1280,80]{1,2,0:T(8,128)(2,1)} %collective-permute-done.8), channel_id=1, source_target_pairs={{0,8},{8,0},{16,24},{24,16},{1,9},{9,1},{17,25},{25,17},{2,10},{10... | collective-permute-start | bytes 5529608 | tf_op jit(solution)/shard_map/ppermute | solution.py:24
  61.5 8.9 %copy-start.6 = (f32[1280]{0:T(1024)S(1)}, f32[1280]{0:T(1024)}, u32[]{:S(2)}) copy-start(f32[1280]{0:T(1024)} %param.13) | copy-start | bytes 15364
  61.6 8.9 %copy-start.7 = (f32[1280]{0:T(1024)S(1)}, f32[1280]{0:T(1024)}, u32[]{:S(2)}) copy-start(f32[1280]{0:T(1024)} %param.12) | copy-start | bytes 15364
  62.6 6.2 %collective-permute-start.4 = (f32[1,32]{1,0:T(1,128)S(1)}, f32[1,32]{1,0:T(1,128)S(1)}, u32[]{:S(2)}, u32[]{:S(2)}) collective-permute-start(f32[1,32]{1,0:T(1,128)S(1)} %bitcast.227), channel_id=1, source_target_pairs={{0,1},{1,0},{2,3},{3,2},{4,5},{5,4},{6,7},{7,6},{8,9},{9,8},{10,11... | collective-permute-start | bytes 392 | tf_op jit(solution)/shard_map/ppermute | solution.py:13
  64.0 6.0 %collective-permute-start.5 = (f32[1,32]{1,0:T(1,128)S(1)}, f32[1,32]{1,0:T(1,128)S(1)}, u32[]{:S(2)}, u32[]{:S(2)}) collective-permute-start(f32[1,32]{1,0:T(1,128)S(1)} %bitcast.228), channel_id=1, source_target_pairs={{0,1},{1,0},{2,3},{3,2},{4,5},{5,4},{6,7},{7,6},{8,9},{9,8},{10,11... | collective-permute-start | bytes 392 | tf_op jit(solution)/shard_map/ppermute | solution.py:13
  64.9 7.7 %collective-permute-start.3 = (bf16[1,4,1,32,1280]{4,3,2,1,0:T(8,128)(2,1)S(1)}, bf16[1,4,1,32,1280]{4,3,2,1,0:T(8,128)(2,1)}, u32[]{:S(2)}, u32[]{:S(2)}) collective-permute-start(bf16[1,4,1,32,1280]{4,3,2,1,0:T(8,128)(2,1)S(1)} %get-tuple-element.31), channel_id=1, source_target_pairs={{0,1},{2,3},{4,5},{6,7},{8,9},{10,11},{12,13},{14,15},{16,17},{18,... | collective-permute-start | bytes 983048 | tf_op jit(solution)/shard_map/ppermute | solution.py:117
  68.8 9.1 %collective-permute-start.6 = (bf16[1,4,1,32,1280]{4,3,2,1,0:T(8,128)(2,1)S(1)}, bf16[1,4,1,32,1280]{4,3,2,1,0:T(8,128)(2,1)}, u32[]{:S(2)}, u32[]{:S(2)}) collective-permute-start(bf16[1,4,1,32,1280]{4,3,2,1,0:T(8,128)(2,1)S(1)} %get-tuple-element.32), channel_id=1, source_target_pairs={{1,0},{3,2},{5,4},{7,6},{9,8},{11,10},{13,12},{15,14},{17,16},{19,... | collective-permute-start | bytes 983048 | tf_op jit(solution)/shard_map/ppermute | solution.py:118
  105.2 3.6 %collective-permute-start.10 = (f32[8]{0:T(128)S(1)}, f32[8]{0:T(128)S(1)}, u32[]{:S(2)}, u32[]{:S(2)}) collective-permute-start(f32[8]{0:T(128)S(1)} %reduce_sum.78), channel_id=1, source_target_pairs={{0,1},{1,0},{2,3},{3,2},{4,5},{5,4},{6,7},{7,6},{8,9},{9,8},{10,11... | collective-permute-start | bytes 104 | tf_op jit(solution)/shard_map/ppermute | solution.py:13
  105.5 3.6 %collective-permute-start.11 = (f32[8]{0:T(128)S(1)}, f32[8]{0:T(128)S(1)}, u32[]{:S(2)}, u32[]{:S(2)}) collective-permute-start(f32[8]{0:T(128)S(1)} %reduce_sum.81), channel_id=1, source_target_pairs={{0,1},{1,0},{2,3},{3,2},{4,5},{5,4},{6,7},{7,6},{8,9},{9,8},{10,11... | collective-permute-start | bytes 104 | tf_op jit(solution)/shard_map/ppermute | solution.py:13
  110.9 10.3 %collective-permute-start.13 = (bf16[3,1280,80]{1,2,0:T(8,128)(2,1)S(1)}, bf16[3,1280,80]{1,2,0:T(8,128)(2,1)}, u32[]{:S(2)}, u32[]{:S(2)}) collective-permute-start(bf16[3,1280,80]{1,2,0:T(8,128)(2,1)S(1)} %copy-done.5), channel_id=1, source_target_pairs={{0,16},{8,24},{16,0},{24,8},{1,17},{9,25},{17,1},{25,9},{2,18},{10... | collective-permute-start | bytes 1843208 | tf_op jit(solution)/shard_map/ppermute | solution.py:22
  112.4 11.0 %collective-permute-start.12 = (bf16[3,1280,80]{1,2,0:T(8,128)(2,1)S(1)}, bf16[3,1280,80]{1,2,0:T(8,128)(2,1)}, u32[]{:S(2)}, u32[]{:S(2)}) collective-permute-start(bf16[3,1280,80]{1,2,0:T(8,128)(2,1)S(1)} %copy-done.5), channel_id=1, source_target_pairs={{0,8},{8,0},{16,24},{24,16},{1,9},{9,1},{17,25},{25,17},{2,10},{10... | collective-permute-start | bytes 1843208 | tf_op jit(solution)/shard_map/ppermute | solution.py:23
  121.2 3.8 %collective-permute-start.14 = (bf16[3,1280,80]{1,2,0:T(8,128)(2,1)}, bf16[3,1280,80]{1,2,0:T(8,128)(2,1)}, u32[]{:S(2)}, u32[]{:S(2)}) collective-permute-start(bf16[3,1280,80]{1,2,0:T(8,128)(2,1)} %collective-permute-done.13), channel_id=1, source_target_pairs={{0,8},{8,0},{16,24},{24,16},{1,9},{9,1},{17,25},{25,17},{2,10},{10... | collective-permute-start | bytes 1843208 | tf_op jit(solution)/shard_map/ppermute | solution.py:24
  183.8 16.4 %collective-permute-start.15 = (bf16[1,8,32,320]{3,2,1,0:T(8,128)(2,1)}, bf16[1,8,32,320]{3,2,1,0:T(8,128)(2,1)S(1)}, u32[]{:S(2)}, u32[]{:S(2)}) collective-permute-start(bf16[1,8,32,320]{3,2,1,0:T(8,128)(2,1)} %get-tuple-element.35), channel_id=1, source_target_pairs={{0,2},{2,4},{4,6},{6,0},{1,3},{3,5},{5,7},{7,1},{8,10},{10,12},{12... | collective-permute-start | bytes 491528 | tf_op jit(solution)/shard_map/ppermute | solution.py:224
  183.9 28.2 %collective-permute-start.16 = (bf16[1,8,32,320]{3,2,1,0:T(8,128)(2,1)}, bf16[1,8,32,320]{3,2,1,0:T(8,128)(2,1)S(1)}, u32[]{:S(2)}, u32[]{:S(2)}) collective-permute-start(bf16[1,8,32,320]{3,2,1,0:T(8,128)(2,1)} %get-tuple-element.34), channel_id=1, source_target_pairs={{0,4},{2,6},{4,0},{6,2},{1,5},{3,7},{5,1},{7,3},{8,12},{10,14},{12... | collective-permute-start | bytes 491528 | tf_op jit(solution)/shard_map/ppermute | solution.py:224
  185.2 38.7 %collective-permute-start.17 = (bf16[1,8,32,320]{3,2,1,0:T(8,128)(2,1)S(1)}, bf16[1,8,32,320]{3,2,1,0:T(8,128)(2,1)S(1)}, u32[]{:S(2)}, u32[]{:S(2)}) collective-permute-start(bf16[1,8,32,320]{3,2,1,0:T(8,128)(2,1)S(1)} %get-tuple-element.33), channel_id=1, source_target_pairs={{0,6},{2,0},{4,2},{6,4},{1,7},{3,1},{5,3},{7,5},{8,14},{10,8},{12,... | collective-permute-start | bytes 491528 | tf_op jit(solution)/shard_map/ppermute | solution.py:224
  224.2 13.7 %copy-start.8 = (f32[1280]{0:T(1024)S(1)}, f32[1280]{0:T(1024)}, u32[]{:S(2)}) copy-start(f32[1280]{0:T(1024)} %param.17) | copy-start | bytes 15364
  (4 other events, 11.9 us)
Sparse Core Ops, SparseCore 0:
  111.0 62.1 all-gather.2
